TPU v7x, 128 devices: a whole 4x4x4 slice. The times are simulated.
128 devices in a mesh: req: 8 (over z, core), mp: 16 (over x, y).
Axes of the slice: x: 4, y: 4, z: 4, core: 2. Of those that a mesh axis runs over, the one named last changes fastest.
Arguments:
- states: bfloat16 [8, 32, 16, 5120], P('req', None, 'mp'), may hold values from -6 to 6
- lengths: int32 [8, 4], replicated, may hold values from 1 to 509, as said below
- request_adapters: int32 [8, 4], replicated, may hold values from 0 to 7
- attention_norm_gain: float32 [5120], replicated, may hold values from 0.1 to 1.9
- query_weight: bfloat16 [5120, 4096], P(None, 'mp')
- key_weight: bfloat16 [5120, 1024], P(None, 'mp')
- value_weight: bfloat16 [5120, 1024], P(None, 'mp'), may hold values from -0.078125 to 0.078125
- output_weight: bfloat16 [4096, 5120], P('mp'), may hold values from -0.09375 to 0.09375
- adapter_down_attention: bfloat16 [5120, 384], replicated, may hold values from -0.078125 to 0.078125
- adapter_up_query: bfloat16 [128, 4096], P(None, 'mp'), may hold values from -0.5 to 0.5
- adapter_up_key_value: bfloat16 [2, 128, 1024], P(None, None, 'mp'), may hold values from -0.5 to 0.5
- adapter_down_output: bfloat16 [4096, 128], P('mp'), may hold values from -0.09375 to 0.09375
- adapter_up_output: bfloat16 [128, 5120], replicated, may hold values from -0.875 to 0.875
- feed_norm_gain: float32 [5120], replicated, may hold values from 0.1 to 1.9
- gate_up_weight: bfloat16 [2, 5120, 10240], P(None, 'req', 'mp'), may hold values from -0.078125 to 0.078125
- down_weight: bfloat16 [5120, 10240], P('req', 'mp'), may hold values from -0.0625 to 0.0625
- adapter_down_gate_up: bfloat16 [5120, 256], replicated, may hold values from -0.078125 to 0.078125
- adapter_up_gate_up: bfloat16 [2, 128, 10240], P(None, None, 'mp'), may hold values from -0.5 to 0.5
- adapter_down_feed: bfloat16 [10240, 128], P('mp'), may hold values from -0.0625 to 0.0625
- adapter_up_feed: bfloat16 [128, 5120], replicated, may hold values from -0.875 to 0.875
Outputs:
- layer_out: bfloat16 [8, 32, 16, 5120], P('req', None, 'mp')
Inputs may be any that keep to these rules, and one draw needn't show every extreme that they name: `lengths`: each request has at least one token; each row sums to at most 512, some row to exactly 512, and all rows together to exactly 2048; some request is 509 tokens long.
All inputs are finite; a program needn't handle non-finite values.
Results may differ from a plain program's by a relative error of at most 0.03.
Values may be sent and summed in bfloat16 or wider, within the bound.
No kernel may reach another device: no remote copies, remote signals or barrier semaphores. Data moves between devices by JAX's collectives and lax.ppermute only.
A program may use at most 128 MiB of HBM per device.

v0:
```python
import jax
import jax.numpy as jnp
from jax import lax
from jax.sharding import PartitionSpec as P

HEAD_SIZE = 128
ADAPTER_RANK = 16
WINDOW = 128
SINK = 4
EPSILON = 1e-05
ROPE_THETA = 1000000.0


def from_partner(shard, axis, stride):
    return lax.ppermute(shard, axis, [(i, i ^ 1 << stride) for i in range(lax.axis_size(axis))])


def slot_info(length_rows, adapter_rows, slot_ids):
    request_ends = jnp.cumsum(length_rows, axis=1, dtype=jnp.int32)
    starts = request_ends - length_rows
    count_req = length_rows.shape[1]
    request = jnp.sum(
        (slot_ids[:, None] >= request_ends).astype(jnp.int32), axis=1, dtype=jnp.int32
    )
    living = request < count_req
    matches = request[:, None] == jnp.arange(count_req, dtype=jnp.int32)[None, :]
    opening = jnp.sum(jnp.where(matches, starts, 0), axis=1, dtype=jnp.int32)
    position = jnp.where(living, slot_ids - opening, 0)
    segment = jnp.where(living, request, count_req + slot_ids)
    chosen = jnp.sum(jnp.where(matches, adapter_rows, 0), axis=1, dtype=jnp.int32)
    adapter_slot = jnp.where(living, chosen, -1)
    return (living, position, segment, adapter_slot)


def normalize(input_tokens, gain_vec):
    values = input_tokens.astype(jnp.float32)
    factor = lax.rsqrt(jnp.mean(values * values, axis=-1, keepdims=True) + EPSILON)
    return (values * factor * gain_vec).astype(jnp.bfloat16)


def adapter_select_mask(adapter_slot, adapter_column_count, adapter_rank_size):
    token_owner_request = jnp.arange(adapter_column_count, dtype=jnp.int32) // adapter_rank_size
    return (adapter_slot[:, None] == token_owner_request[None, :]).astype(jnp.float32)


def rotate(vectors, position):
    half_dim = vectors.shape[-1] // 2
    inverse = ROPE_THETA ** (-(jnp.arange(half_dim, dtype=jnp.float32) * (2.0 / vectors.shape[-1])))
    angles = position.astype(jnp.float32)[:, None] * inverse[None, :]
    cosine = jnp.cos(angles)[:, None, :]
    sine_part = jnp.sin(angles)[:, None, :]
    lower_half = vectors[..., :half_dim]
    upper_half = vectors[..., half_dim:]
    return jnp.concatenate(
        [
            lower_half * cosine - upper_half * sine_part,
            upper_half * cosine + lower_half * sine_part,
        ],
        axis=-1,
    )


def attend(queries, key_rows, value_rows, position, segment):
    key_heads = key_rows.shape[1]
    group_size = queries.shape[1] // key_heads
    token_count = queries.shape[0]
    grouped_queries = queries.reshape(token_count, key_heads, group_size, queries.shape[2])
    scores = jnp.einsum(
        "qkgd,skd->kgqs", grouped_queries, key_rows, preferred_element_type=jnp.float32
    ) * queries.shape[2] ** (-0.5)
    allowed = (segment[:, None] == segment[None, :]) & (position[None, :] <= position[:, None])
    allowed = allowed & (
        (position[:, None] - position[None, :] < WINDOW) | (position[None, :] < SINK)
    )
    scores = jnp.where(allowed[None, None], scores, -jnp.inf)
    highest = jnp.max(scores, axis=-1, keepdims=True)
    weights_raw = jnp.exp(scores - highest)
    weights = (weights_raw / jnp.sum(weights_raw, axis=-1, keepdims=True)).astype(jnp.bfloat16)
    blended = jnp.einsum("kgqs,skd->qkgd", weights, value_rows, preferred_element_type=jnp.float32)
    return blended.reshape(token_count, -1).astype(jnp.bfloat16)


def spread_rows(first_part, second_part):
    return (
        lax.all_gather(first_part, "mp", axis=0, tiled=True),
        lax.all_gather(second_part, "mp", axis=0, tiled=True),
    )


def sum_rows(term_fn, row_count):
    return lax.psum_scatter(
        term_fn(jnp.int32(0), lax.axis_size("mp") * row_count).astype(jnp.bfloat16),
        "mp",
        scatter_dimension=0,
        tiled=True,
    ).astype(jnp.float32)


def feed_forward(
    residual_stream,
    adapter_indicator,
    feed_norm_gain,
    adapter_down_gate_up,
    adapter_up_gate_up,
    gate_up_full,
    down_full,
    adapter_down_feed,
    adapter_up_feed,
):
    adapter_column_count = adapter_indicator.shape[1]
    model_width = residual_stream.shape[1]
    feed_input = normalize(residual_stream, feed_norm_gain)
    gate_terms = (
        jnp.dot(feed_input, adapter_down_gate_up, preferred_element_type=jnp.float32)
        * jnp.tile(adapter_indicator, (1, 2))
    ).astype(jnp.bfloat16)
    mlp_all, gate_adapter_ranks = spread_rows(feed_input, gate_terms)
    gate_activation = jnp.dot(
        mlp_all, gate_up_full[0], preferred_element_type=jnp.float32
    ) + jnp.dot(
        gate_adapter_ranks[:, :adapter_column_count],
        adapter_up_gate_up[0],
        preferred_element_type=jnp.float32,
    )
    up_projected = jnp.dot(mlp_all, gate_up_full[1], preferred_element_type=jnp.float32) + jnp.dot(
        gate_adapter_ranks[:, adapter_column_count:],
        adapter_up_gate_up[1],
        preferred_element_type=jnp.float32,
    )
    hidden_activation = (jax.nn.silu(gate_activation) * up_projected).astype(jnp.bfloat16)

    def down_term(first_row, row_count):
        projected_rows = lax.dot_general(
            hidden_activation,
            down_full,
            (((1,), (1,)), ((), ())),
            preferred_element_type=jnp.float32,
        )
        return jnp.concatenate(
            [
                projected_rows,
                jnp.dot(hidden_activation, adapter_down_feed, preferred_element_type=jnp.float32),
            ],
            axis=1,
        )

    summed = sum_rows(down_term, residual_stream.shape[0])
    down_adapter_ranks = (summed[:, model_width:] * adapter_indicator).astype(jnp.bfloat16)
    return (
        residual_stream.astype(jnp.float32)
        + summed[:, :model_width]
        + jnp.dot(down_adapter_ranks, adapter_up_feed, preferred_element_type=jnp.float32)
    )


def shards(
    states,
    lengths,
    request_adapters,
    attention_norm_gain,
    query_weight,
    key_weight,
    value_weight,
    output_weight,
    adapter_down_attention,
    adapter_up_query,
    adapter_up_key_value,
    adapter_down_output,
    adapter_up_output,
    feed_norm_gain,
    gate_up_weight,
    down_weight,
    adapter_down_gate_up,
    adapter_up_gate_up,
    adapter_down_feed,
    adapter_up_feed,
):
    mp_count = lax.axis_size("mp")
    group_index = lax.axis_index("req")
    mp_index = lax.axis_index("mp")
    slot_dev = states.shape[1]
    model_width = states.shape[3]
    adapter_column_count = adapter_up_output.shape[0]
    total_rows = slot_dev * mp_count
    gate_up_full, down_full = (
        lax.all_gather(gate_up_weight, "req", axis=1, tiled=True),
        lax.all_gather(down_weight, "req", axis=0, tiled=True),
    )
    local_rows = states.reshape(slot_dev, model_width)
    own_lengths = lax.dynamic_index_in_dim(lengths, group_index, 0, keepdims=False)
    own_adapters = lax.dynamic_index_in_dim(request_adapters, group_index, 0, keepdims=False)
    request_count = own_lengths.shape[0]
    local_slots = jnp.arange(slot_dev, dtype=jnp.int32) * mp_count + mp_index
    living, unused_pos, unused_seg, adapter_within = slot_info(
        jnp.broadcast_to(own_lengths[None, :], (slot_dev, request_count)),
        jnp.broadcast_to(own_adapters[None, :], (slot_dev, request_count)),
        local_slots,
    )
    indicator_within = adapter_select_mask(adapter_within, adapter_column_count, ADAPTER_RANK)
    normed_rows = normalize(local_rows, attention_norm_gain)
    down_adapter_terms = (
        jnp.dot(normed_rows, adapter_down_attention, preferred_element_type=jnp.float32)
        * jnp.tile(indicator_within, (1, 3))
    ).astype(jnp.bfloat16)
    normed_all, adapter_terms_all = spread_rows(normed_rows, down_adapter_terms)
    gathered = jnp.arange(total_rows, dtype=jnp.int32)
    gathered_slots = gathered % slot_dev * mp_count + gathered // slot_dev
    ignored, position_all, segment_all, unused = slot_info(
        jnp.broadcast_to(own_lengths[None, :], (total_rows, request_count)),
        jnp.broadcast_to(own_adapters[None, :], (total_rows, request_count)),
        gathered_slots,
    )
    query_projected = jnp.dot(
        normed_all, query_weight, preferred_element_type=jnp.float32
    ) + jnp.dot(
        adapter_terms_all[:, :adapter_column_count],
        adapter_up_query,
        preferred_element_type=jnp.float32,
    )
    key_projected = jnp.dot(normed_all, key_weight, preferred_element_type=jnp.float32) + jnp.dot(
        adapter_terms_all[:, adapter_column_count : 2 * adapter_column_count],
        adapter_up_key_value[0],
        preferred_element_type=jnp.float32,
    )
    value_projected = jnp.dot(
        normed_all, value_weight, preferred_element_type=jnp.float32
    ) + jnp.dot(
        adapter_terms_all[:, 2 * adapter_column_count :],
        adapter_up_key_value[1],
        preferred_element_type=jnp.float32,
    )
    kv_pair = jnp.stack([key_projected, value_projected])
    partner = from_partner(kv_pair.astype(jnp.bfloat16), "mp", 0).astype(kv_pair.dtype)
    parity = mp_index % 2
    joined = jnp.where(
        parity == 0,
        jnp.concatenate([kv_pair, partner], axis=2),
        jnp.concatenate([partner, kv_pair], axis=2),
    )
    key_projected = joined[0]
    value_projected = joined[1]
    queries = rotate(query_projected.reshape(total_rows, -1, HEAD_SIZE), position_all).astype(
        jnp.bfloat16
    )
    key_rows = rotate(key_projected.reshape(total_rows, -1, HEAD_SIZE), position_all).astype(
        jnp.bfloat16
    )
    value_rows = value_projected.reshape(total_rows, -1, HEAD_SIZE).astype(jnp.bfloat16)
    attention_output = attend(queries, key_rows, value_rows, position_all, segment_all)

    def out_term(first_row, row_count):
        return jnp.concatenate(
            [
                jnp.dot(attention_output, output_weight, preferred_element_type=jnp.float32),
                jnp.dot(attention_output, adapter_down_output, preferred_element_type=jnp.float32),
            ],
            axis=1,
        )

    summed = sum_rows(out_term, slot_dev)
    output_adapter_ranks = (summed[:, model_width:] * indicator_within).astype(jnp.bfloat16)
    residual_stream = (
        local_rows.astype(jnp.float32)
        + summed[:, :model_width]
        + jnp.dot(output_adapter_ranks, adapter_up_output, preferred_element_type=jnp.float32)
    ).astype(jnp.bfloat16)
    layer_result = feed_forward(
        residual_stream,
        indicator_within,
        feed_norm_gain,
        adapter_down_gate_up,
        adapter_up_gate_up,
        gate_up_full,
        down_full,
        adapter_down_feed,
        adapter_up_feed,
    )
    finished = jnp.where(living[:, None], layer_result, jnp.zeros_like(layer_result)).astype(
        jnp.bfloat16
    )
    return finished.reshape(1, slot_dev, 1, model_width)


def solution(mesh):
    placed = (
        P("req", None, "mp", None),
        P(),
        P(),
        P(),
        P(None, "mp"),
        P(None, "mp"),
        P(None, "mp"),
        P("mp", None),
        P(),
        P(None, "mp"),
        P(None, None, "mp"),
        P("mp", None),
        P(),
        P(),
        P(None, "req", "mp"),
        P("req", "mp"),
        P(),
        P(None, None, "mp"),
        P("mp", None),
        P(),
    )
    return jax.shard_map(
        shards, mesh=mesh, in_specs=placed, out_specs=P("req", None, "mp", None), check_vma=False
    )
```

profile of v0, /device:TPU:0, one launch (start us, length us, event | category | flops | bytes accessed | tf_op | source)
XLA Modules:
  0.0 374.3 jit_solution(9356517427873892993)
XLA Ops:
  7.4 1.3 fusion.17
  8.7 1.9 fusion.19
  10.6 0.9 dynamic-slice_reduce_fusion
  12.0 0.3 copy-done.21
  12.3 2.9 fusion.12
  15.2 25.0 %all_gather.19 = bf16[512,384]{1,0:T(8,128)(2,1)S(1)} all-gather(bf16[32,384]{1,0:T(8,128)(2,1)S(1)} %fusion.12), channel_id=1, replica_groups=mesh['req'=8,'mp'=16] {'mp'}, dimensions={0}, use_global_device_ids=true | all-gather | bytes 417792 | tf_op jit(solution)/shard_map/all_gather | solution.py:86
  40.4 1.2 fusion.16
  41.6 1.8 multiply_cosine_fusion
  43.4 26.8 %all-gather.5.cloned.1.call-done = bf16[512,5120]{1,0:T(8,128)(2,1)} async-done(((bf16[32,5120]{1,0:T(8,128)(2,1)}), bf16[512,5120]{1,0:T(8,128)(2,1)}) %all-gather.5.cloned.1.call-update) | async-done | bytes 5242896 | tf_op jit(solution)/shard_map/all_gather | solution.py:85
  70.2 4.5 %fusion.76 = f32[512,64]{0,1:T(8,128)S(1)} fusion(bf16[512,5120]{1,0:T(8,128)(2,1)} %all-gather.5.cloned.1.call-done, bf16[5120,64]{0,1:T(8,128)(2,1)} %param.26), kind=kOutput, calls=%fused_computation.140 | convolution fusion | flops 335544320 | bytes 6029312 | tf_op jit(solution)/shard_map/dot_general | solution.py:225
  74.9 1.7 fusion.75
  76.8 0.7 maximum_convert_fusion
  77.5 1.4 collective-permute-start
  78.9 1.6 fusion.77
  80.5 0.3 convolution_add_fusion.4
  80.8 0.8 fusion.73
  81.6 1.1 copy.44
  82.7 1.9 copy.45
  84.7 1.4 subtract_convert_fusion
  86.2 0.6 fusion.45
  86.8 0.6 fusion.74
  87.4 0.3 fusion.7
  87.7 0.5 convolution_convert_fusion.2
  88.3 1.6 convolution_convert_fusion
  89.8 0.3 convolution_convert_fusion.4
  90.1 2.7 pad_maximum_fusion
  92.9 0.5 all-gather.9.cloned.1.call-update
  93.7 78.0 %reduce-scatter.3.cloned.1.call-done = bf16[32,5248]{1,0:T(8,128)(2,1)} async-done(((bf16[512,5248]{1,0:T(8,128)(2,1)}), bf16[32,5248]{1,0:T(8,128)(2,1)}) %reduce-scatter.3.cloned.1.call-update) | async-done | bytes 335888 | tf_op jit(solution)/shard_map/reduce_scatter | solution.py:91
  171.7 1.0 convert_element_type.118
  172.8 0.5 multiply_reduce_fusion
  173.3 0.9 multiply_convert_fusion
  174.2 0.5 all-gather.11.cloned.1.call-update
  174.8 2.4 fusion.13
  177.2 23.4 %all_gather.22 = bf16[512,256]{1,0:T(8,128)(2,1)S(1)} all-gather(bf16[32,256]{1,0:T(8,128)(2,1)S(1)} %fusion.13), channel_id=1, replica_groups=mesh['req'=8,'mp'=16] {'mp'}, dimensions={0}, use_global_device_ids=true | all-gather | bytes 278528 | tf_op jit(solution)/shard_map/all_gather | solution.py:86
  200.7 29.8 %all-gather.7.cloned.1.call-done = bf16[512,5120]{1,0:T(8,128)(2,1)} async-done(((bf16[32,5120]{1,0:T(8,128)(2,1)}), bf16[512,5120]{1,0:T(8,128)(2,1)}) %all-gather.7.cloned.1.call-update) | async-done | bytes 5242896 | tf_op jit(solution)/shard_map/all_gather | solution.py:85
  230.5 8.7 %fusion.1 = f32[512,640]{1,0:T(8,128)S(1)} fusion(bf16[512,5120]{1,0:T(8,128)(2,1)} %all-gather.7.cloned.1.call-done, bf16[2,5120,640]{2,1,0:T(8,128)(2,1)} %all-gather.9.cloned.1.call-done), kind=kOutput, calls=%fused_computation.5 | convolution fusion | flops 3355443200 | bytes 13107200 | tf_op jit(solution)/shard_map/dot_general | solution.py:118
  239.2 1.2 convolution_add_fusion.3
  240.5 4.3 %fusion = f32[512,640]{1,0:T(8,128)S(1)} fusion(bf16[512,5120]{1,0:T(8,128)(2,1)S(1)} %copy-done.24, bf16[2,5120,640]{2,1,0:T(8,128)(2,1)S(1)} %copy-done.23), kind=kOutput, calls=%fused_computation.3 | convolution fusion | flops 3355443200 | bytes 13107200 | tf_op jit(solution)/shard_map/dot_general | solution.py:125
  244.8 0.5 fusion.9
  245.3 0.4 copy-done.7
  245.7 0.3 convolution_convert_fusion.3
  246.0 27.8 %all-gather.11.cloned.1.call-done = bf16[5120,640]{1,0:T(8,128)(2,1)} async-done(((bf16[640,640]{1,0:T(8,128)(2,1)}), bf16[5120,640]{1,0:T(8,128)(2,1)}) %all-gather.11.cloned.1.call-update) | async-done | bytes 6553616 | tf_op jit(solution)/shard_map/all_gather | solution.py:187
  273.9 7.3 %convolution_convert_fusion.1 = bf16[512,5120]{1,0:T(8,128)(2,1)S(1)} fusion(bf16[512,640]{1,0:T(8,128)(2,1)S(1)} %fusion.9, bf16[5120,640]{1,0:T(8,128)(2,1)} %all-gather.11.cloned.1.call-done), kind=kOutput, calls=%fused_computation.1 | convolution fusion | flops 3358064640 | bytes 12451840 | tf_op jit(solution)/shard_map/dot_general | solution.py:133
  281.2 2.7 pad_maximum_fusion.1
  283.9 0.6 copy-done.22
  284.6 79.0 %reduce-scatter.5.cloned.1.call-done = bf16[32,5248]{1,0:T(8,128)(2,1)} async-done(((bf16[512,5248]{1,0:T(8,128)(2,1)}), bf16[32,5248]{1,0:T(8,128)(2,1)}) %reduce-scatter.5.cloned.1.call-update) | async-done | bytes 335888 | tf_op jit(solution)/shard_map/reduce_scatter | solution.py:91
  363.5 1.0 convert_element_type.125
  364.5 2.4 fusion.6
  (87 shorter events, 1.6 us)
Async XLA Ops:
  7.4 80.9 %copy-start = (bf16[256,5120]{1,0:T(8,128)(2,1)S(1)}, bf16[256,5120]{1,0:T(8,128)(2,1)}, u32[]{:S(2)}) copy-start(bf16[256,5120]{1,0:T(8,128)(2,1)} %param.27) | copy-start | bytes 7864324
  7.4 62.8 %all-gather.5.cloned.1.call-start = ((), (), s32[]{:S(2)}) async-start(), calls=%async_computation.2 | async-start | bytes 5570560 | tf_op jit(solution)/shard_map/all_gather | solution.py:85
  10.6 161.2 %reduce-scatter.3.cloned.1.call-start = ((), (), s32[]{:S(2)}) async-start(), calls=%async_computation.3 | async-start | bytes 5709824 | tf_op jit(solution)/shard_map/reduce_scatter | solution.py:91
  11.8 31.6 %copy-start.15 = (s32[128]{0:T(128)}, s32[128]{0:T(128)S(1)}, u32[]{:S(2)}) copy-start(s32[128]{0:T(128)S(1)} %and_select_fusion) | copy-start | bytes 1540
  11.8 0.5 copy-start.21
  11.9 31.5 %copy-start.17 = (s32[32]{0:T(128)}, s32[32]{0:T(128)S(1)}, u32[]{:S(2)}) copy-start(s32[32]{0:T(128)S(1)} %broadcast_select_fusion) | copy-start | bytes 388
  40.3 3.1 copy-start.19
  40.4 3.0 copy-start.13
  43.4 31.3 %copy-start.11 = (bf16[2,128,64]{1,2,0:T(8,128)(2,1)S(1)}, bf16[2,128,64]{1,2,0:T(8,128)(2,1)}, u32[]{:S(2)}) copy-start(bf16[2,128,64]{1,2,0:T(8,128)(2,1)} %param.30) | copy-start | bytes 98308
  70.2 4.7 %copy-start.2 = (bf16[512,5120]{1,0:T(8,128)(2,1)S(1)}, bf16[512,5120]{1,0:T(8,128)(2,1)}, u32[]{:S(2)}) copy-start(bf16[512,5120]{1,0:T(8,128)(2,1)} %all-gather.5.cloned.1.call-done) | copy-start | bytes 15728644
  70.2 4.7 %copy-start.5 = (bf16[5120,64]{0,1:T(8,128)(2,1)S(1)}, bf16[5120,64]{0,1:T(8,128)(2,1)}, u32[]{:S(2)}) copy-start(bf16[5120,64]{0,1:T(8,128)(2,1)} %param.25) | copy-start | bytes 1966084
  74.9 4.0 %copy-start.25 = (bf16[5120,256]{1,0:T(8,128)(2,1)S(1)}, bf16[5120,256]{1,0:T(8,128)(2,1)}, u32[]{:S(2)}) copy-start(bf16[5120,256]{1,0:T(8,128)(2,1)} %param.24) | copy-start | bytes 7864324
  77.5 3.0 copy-start.9
  77.5 8.6 %collective-permute-start = (bf16[2,512,64]{1,2,0:T(8,128)(2,1)}, bf16[2,512,64]{1,2,0:T(8,128)(2,1)S(1)}, u32[]{:S(2)}, u32[]{:S(2)}) collective-permute-start(bf16[2,512,64]{1,2,0:T(8,128)(2,1)} %maximum_convert_fusion), channel_id=1, source_target_pairs={{0,1},{1,0},{2,3},{3,2},{4,5},{5,4},{6,7},{7,6},{8,9},{9,8},{10,11... | collective-permute-start | bytes 393224 | tf_op jit(solution)/shard_map/ppermute | solution.py:15
  84.7 1.5 copy-start.14
  84.7 1.5 copy-start.20
  84.7 2.1 copy-start.6
  88.3 1.6 copy-start.10
  92.8 79.9 %copy-start.3 = (bf16[1,32,1,5120]{3,1,2,0:T(8,128)(2,1)S(1)}, bf16[1,32,1,5120]{3,1,2,0:T(8,128)(2,1)}, u32[]{:S(2)}) copy-start(bf16[1,32,1,5120]{3,1,2,0:T(8,128)(2,1)} %param.20) | copy-start | bytes 983044
  92.8 79.9 %copy-start.4 = (bf16[128,5120]{1,0:T(8,128)(2,1)S(1)}, bf16[128,5120]{1,0:T(8,128)(2,1)}, u32[]{:S(2)}) copy-start(bf16[128,5120]{1,0:T(8,128)(2,1)} %param.32) | copy-start | bytes 3932164
  92.9 79.9 %copy-start.16 = (s32[128]{0:T(128)S(1)}, s32[128]{0:T(128)}, u32[]{:S(2)}) copy-start(s32[128]{0:T(128)} %copy-done.15) | copy-start | bytes 1540
  92.9 79.9 %copy-start.18 = (s32[32]{0:T(128)S(1)}, s32[32]{0:T(128)}, u32[]{:S(2)}) copy-start(s32[32]{0:T(128)} %copy-done.17) | copy-start | bytes 388
  92.9 80.4 %copy-start.12 = (f32[5120]{0:T(1024)S(1)}, f32[5120]{0:T(1024)}, u32[]{:S(2)}) copy-start(f32[5120]{0:T(1024)} %param.33) | copy-start | bytes 61444
  92.9 107.8 %all-gather.9.cloned.1.call-start = ((), (), s32[]{:S(2)}) async-start(), calls=%async_computation.5 | async-start | bytes 14745600 | tf_op jit(solution)/shard_map/all_gather | solution.py:186
  93.5 137.0 %all-gather.7.cloned.1.call-start = ((), (), s32[]{:S(2)}) async-start(), calls=%async_computation.4 | async-start | bytes 5570560 | tf_op jit(solution)/shard_map/all_gather | solution.py:85
  174.2 99.7 %all-gather.11.cloned.1.call-start = ((), (), s32[]{:S(2)}) async-start(), calls=%async_computation.6 | async-start | bytes 7372800 | tf_op jit(solution)/shard_map/all_gather | solution.py:187
  174.7 188.8 %reduce-scatter.5.cloned.1.call-start = ((), (), s32[]{:S(2)}) async-start(), calls=%async_computation.7 | async-start | bytes 5709824 | tf_op jit(solution)/shard_map/reduce_scatter | solution.py:91
  230.5 10.0 %copy-start.23 = (bf16[2,5120,640]{2,1,0:T(8,128)(2,1)S(1)}, bf16[2,5120,640]{2,1,0:T(8,128)(2,1)}, u32[]{:S(2)}) copy-start(bf16[2,5120,640]{2,1,0:T(8,128)(2,1)} %all-gather.9.cloned.1.call-done) | copy-start | bytes 39321604
  230.5 10.0 %copy-start.24 = (bf16[512,5120]{1,0:T(8,128)(2,1)S(1)}, bf16[512,5120]{1,0:T(8,128)(2,1)}, u32[]{:S(2)}) copy-start(bf16[512,5120]{1,0:T(8,128)(2,1)} %all-gather.7.cloned.1.call-done) | copy-start | bytes 15728644
  240.5 4.3 %copy-start.8 = (bf16[2,128,640]{2,1,0:T(8,128)(2,1)S(1)}, bf16[2,128,640]{2,1,0:T(8,128)(2,1)}, u32[]{:S(2)}) copy-start(bf16[2,128,640]{2,1,0:T(8,128)(2,1)} %param.37) | copy-start | bytes 983044
  244.8 0.9 copy-start.7
  283.9 0.6 copy-start.22
  284.5 82.4 %copy-start.1 = (bf16[256,5120]{1,0:T(8,128)(2,1)S(1)}, bf16[256,5120]{1,0:T(8,128)(2,1)}, u32[]{:S(2)}) copy-start(bf16[256,5120]{1,0:T(8,128)(2,1)} %param.27) | copy-start | bytes 7864324
Sparse Core Ops, SparseCore 0:
  10.7 59.4 all-gather.4
  93.0 78.7 reduce-scatter.2
  284.1 79.3 reduce-scatter.4
Sparse Core Ops, SparseCore 1:
  95.1 69.0 all-gather.8
  174.2 56.2 all-gather.6
  232.0 41.8 all-gather.10
where the time goes:
time: 375 us; the launch traced here: 374 us
  waiting for transfers between devices  243 us (65%)
  blocking collectives  48.4 us (13%)
  matrix products  41.9 us (11%)
  other arithmetic  17.8 us (5%)
  between operations  15.3 us (4%)
  local copies, waits for them, and re-layouts  6.46 us (2%)
    reduce_scatter x2, waiting for transfers between devices, sum_rows(): lax.psum_scatter(term_fn(jnp.int32(0), lax.axis_size('mp') * row_count).a...  157 us
    all_gather x2, waiting for transfers between devices, spread_rows(): lax.all_gather(first_part, 'mp', axis=0, tiled=True)  56.6 us
    all_gather x2, blocking collectives, spread_rows(): lax.all_gather(second_part, 'mp', axis=0, tiled=True)  48.4 us
    all_gather x1, waiting for transfers between devices, shards(): lax.all_gather(down_weight, 'req', axis=0, tiled=True)  27.8 us
    dot_general x1, matrix products, feed_forward(): jnp.dot(mlp_all, gate_up_full[0], preferred_element_type=jnp.float32)  8.72 us
  transfers between devices with their start and end apart: 7, of which 5 were waited for; matrix products, arithmetic and copies ran while one was open for 9% of the time, Pallas kernels for 0%

commit v1 on v0

--- a/solution.py
+++ b/solution.py
@@ -9,6 +9,19 @@
 SINK = 4
 EPSILON = 1e-05
 ROPE_THETA = 1000000.0
+
+
+def ring_gather(x, axis, dim):
+    ways = lax.axis_size(axis)
+    up = [(d, (d + 1) % ways) for d in range(ways)]
+    down = [(d, (d - 1) % ways) for d in range(ways)]
+    earlier, later = ([x], [x])
+    for _ in range(ways // 2):
+        earlier.append(lax.ppermute(earlier[-1], axis, up))
+    for _ in range((ways - 1) // 2):
+        later.append(lax.ppermute(later[-1], axis, down))
+    line = jnp.concatenate([*earlier[::-1], *later[1:]], axis=dim)
+    return jnp.roll(line, (lax.axis_index(axis) - ways // 2) * x.shape[dim], axis=dim)
 
 
 def from_partner(shard, axis, stride):
@@ -81,10 +94,7 @@
 
 
 def spread_rows(first_part, second_part):
-    return (
-        lax.all_gather(first_part, "mp", axis=0, tiled=True),
-        lax.all_gather(second_part, "mp", axis=0, tiled=True),
-    )
+    return (ring_gather(first_part, "mp", 0), lax.all_gather(second_part, "mp", axis=0, tiled=True))
 
 
 def sum_rows(term_fn, row_count):

time: 375 us -> 483 us (1.29); the launches traced: 374 us -> 475 us
  starting transfers between devices: 1.82 us -> 74.3 us
  local copies, waits for them, and re-layouts: 6.46 us -> 29.9 us
  waiting for transfers between devices: 243 us -> 233 us
  other arithmetic: 17.8 us -> 23.7 us
    ppermute x0 -> x30, waiting for transfers between devices: none -> 78.2 us  [the longest x16 64 us: ring_gather(): earlier.append(lax.ppermute(earlier[-1], axis, up))]
    ppermute x0 -> x30, starting transfers between devices: none -> 74 us  [the longest x14 70.2 us: ring_gather(): later.append(lax.ppermute(later[-1], axis, down))]
    all_gather x2 -> x0, waiting for transfers between devices: 56.6 us -> none  [spread_rows(): lax.all_gather(first_part, 'mp', axis=0, tiled=True)]
    all_gather x1, waiting for transfers between devices: 27.8 us -> 0.03 us  [shards(): lax.all_gather(down_weight, 'req', axis=0, tiled=True)]
    unnamed x54 -> x126, local copies, waits for them, and re-layouts: 4.53 us -> 27.2 us
    concatenate x0 -> x1, other arithmetic: none -> 4.88 us  [ring_gather(): jnp.roll(line, (lax.axis_index(axis) - ways // 2) * x.shape[dim], axis=dim)]
  transfers between devices with their start and end apart: 7 -> 35, of which waited for: 5 -> 17; matrix products, arithmetic and copies ran while one was open for 9% -> 14% of each run, Pallas kernels for 0% -> 0%
where the time goes in v1:
time: 483 us; the launch traced here: 475 us
  waiting for transfers between devices  233 us (48%)
  starting transfers between devices  74.3 us (15%)
  blocking collectives  52.6 us (11%)
  matrix products  46 us (10%)
  local copies, waits for them, and re-layouts  29.9 us (6%)
  other arithmetic  23.7 us (5%)
  between operations  15.9 us (3%)
    reduce_scatter x2, waiting for transfers between devices, sum_rows(): lax.psum_scatter(term_fn(jnp.int32(0), lax.axis_size('mp') * row_count).a...  154 us
    ppermute x14, starting transfers between devices, ring_gather(): later.append(lax.ppermute(later[-1], axis, down))  70.2 us
    ppermute x16, waiting for transfers between devices, ring_gather(): earlier.append(lax.ppermute(earlier[-1], axis, up))  64 us
    all_gather x2, blocking collectives, spread_rows(): lax.all_gather(second_part, 'mp', axis=0, tiled=True)  52.6 us
    unnamed x126, local copies, waits for them, and re-layouts  27.2 us
    ppermute x14, waiting for transfers between devices, ring_gather(): later.append(lax.ppermute(later[-1], axis, down))  14.2 us
  transfers between devices with their start and end apart: 35, of which 17 were waited for; matrix products, arithmetic and copies ran while one was open for 14% of the time, Pallas kernels for 0%

profile of v1, /device:TPU:0, one launch (start us, length us, event | category | flops | bytes accessed | tf_op | source)
XLA Modules:
  0.0 475.4 jit_solution(12769355649864329331)
XLA Ops:
  9.8 1.7 collective-permute-start
  11.6 3.7 collective-permute-start.8
  16.6 6.3 %collective-permute-done = bf16[32,5120]{1,0:T(8,128)(2,1)S(1)} collective-permute-done((bf16[32,5120]{1,0:T(8,128)(2,1)S(1)}, bf16[32,5120]{1,0:T(8,128)(2,1)S(1)}, u32[]{:S(2)}, u32[]{:S(2)}) %collective-permute-start) | collective-permute-done | bytes 327712 | tf_op jit(solution)/shard_map/ppermute | solution.py:20
  23.0 12.1 %collective-permute-done.1 = bf16[32,5120]{1,0:T(8,128)(2,1)S(1)} collective-permute-done((bf16[32,5120]{1,0:T(8,128)(2,1)S(1)}, bf16[32,5120]{1,0:T(8,128)(2,1)S(1)}, u32[]{:S(2)}, u32[]{:S(2)}) %collective-permute-start.1) | collective-permute-done | bytes 327712 | tf_op jit(solution)/shard_map/ppermute | solution.py:20
  35.1 5.4 %collective-permute-start.9 = (bf16[32,5120]{1,0:T(8,128)(2,1)}, bf16[32,5120]{1,0:T(8,128)(2,1)S(1)}, u32[]{:S(2)}, u32[]{:S(2)}) collective-permute-start(bf16[32,5120]{1,0:T(8,128)(2,1)} %collective-permute-done.8), channel_id=1, source_target_pairs={{0,15},{1,0},{2,1},{3,2},{4,3},{5,4},{6,5},{7,6},{8,7},{9,8},{10,9... | collective-permute-start | bytes 983048 | tf_op jit(solution)/shard_map/ppermute | solution.py:22
  40.5 5.8 %collective-permute-done.2 = bf16[32,5120]{1,0:T(8,128)(2,1)S(1)} collective-permute-done((bf16[32,5120]{1,0:T(8,128)(2,1)S(1)}, bf16[32,5120]{1,0:T(8,128)(2,1)S(1)}, u32[]{:S(2)}, u32[]{:S(2)}) %collective-permute-start.2) | collective-permute-done | bytes 327712 | tf_op jit(solution)/shard_map/ppermute | solution.py:20
  46.4 2.9 fusion.14
  49.3 5.3 %collective-permute-start.10 = (bf16[32,5120]{1,0:T(8,128)(2,1)S(1)}, bf16[32,5120]{1,0:T(8,128)(2,1)S(1)}, u32[]{:S(2)}, u32[]{:S(2)}) collective-permute-start(bf16[32,5120]{1,0:T(8,128)(2,1)S(1)} %collective-permute-done.9), channel_id=1, source_target_pairs={{0,15},{1,0},{2,1},{3,2},{4,3},{5,4},{6,5},{7,6},{8,7},{9,8},{10,9... | collective-permute-start | bytes 983048 | tf_op jit(solution)/shard_map/ppermute | solution.py:22
  54.6 2.1 collective-permute-done.3
  56.7 25.8 %all_gather.12 = bf16[512,384]{1,0:T(8,128)(2,1)S(1)} all-gather(bf16[32,384]{1,0:T(8,128)(2,1)S(1)} %fusion.14), channel_id=1, replica_groups=mesh['req'=8,'mp'=16] {'mp'}, dimensions={0}, use_global_device_ids=true | all-gather | bytes 417792 | tf_op jit(solution)/shard_map/all_gather | solution.py:97
  82.7 4.6 collective-permute-start.11
  88.2 5.6 %collective-permute-done.11 = bf16[32,5120]{1,0:T(8,128)(2,1)S(1)} collective-permute-done((bf16[32,5120]{1,0:T(8,128)(2,1)S(1)}, bf16[32,5120]{1,0:T(8,128)(2,1)S(1)}, u32[]{:S(2)}, u32[]{:S(2)}) %collective-permute-start.11) | collective-permute-done | bytes 327712 | tf_op jit(solution)/shard_map/ppermute | solution.py:22
  93.8 5.8 %collective-permute-start.12 = (bf16[32,5120]{1,0:T(8,128)(2,1)S(1)}, bf16[32,5120]{1,0:T(8,128)(2,1)}, u32[]{:S(2)}, u32[]{:S(2)}) collective-permute-start(bf16[32,5120]{1,0:T(8,128)(2,1)S(1)} %collective-permute-done.11), channel_id=1, source_target_pairs={{0,15},{1,0},{2,1},{3,2},{4,3},{5,4},{6,5},{7,6},{8,7},{9,8},{10,9... | collective-permute-start | bytes 983048 | tf_op jit(solution)/shard_map/ppermute | solution.py:22
  99.8 1.8 multiply_cosine_fusion
  101.6 3.9 collective-permute-done.12
  105.5 5.9 %collective-permute-start.13 = (bf16[32,5120]{1,0:T(8,128)(2,1)}, bf16[32,5120]{1,0:T(8,128)(2,1)}, u32[]{:S(2)}, u32[]{:S(2)}) collective-permute-start(bf16[32,5120]{1,0:T(8,128)(2,1)} %collective-permute-done.12), channel_id=1, source_target_pairs={{0,15},{1,0},{2,1},{3,2},{4,3},{5,4},{6,5},{7,6},{8,7},{9,8},{10,9... | collective-permute-start | bytes 983048 | tf_op jit(solution)/shard_map/ppermute | solution.py:22
  112.5 2.0 fusion.43
  114.6 2.4 collective-permute-done.13
  117.0 6.2 %collective-permute-start.14 = (bf16[32,5120]{1,0:T(8,128)(2,1)}, bf16[32,5120]{1,0:T(8,128)(2,1)S(1)}, u32[]{:S(2)}, u32[]{:S(2)}) collective-permute-start(bf16[32,5120]{1,0:T(8,128)(2,1)} %collective-permute-done.13), channel_id=1, source_target_pairs={{0,15},{1,0},{2,1},{3,2},{4,3},{5,4},{6,5},{7,6},{8,7},{9,8},{10,9... | collective-permute-start | bytes 983048 | tf_op jit(solution)/shard_map/ppermute | solution.py:22
  134.2 4.9 %fusion.8 = bf16[512,5120]{1,0:T(8,128)(2,1)S(1)} fusion(s32[]{:T(128)S(6)} %select_n.173, bf16[512,5120]{1,0:T(8,128)(2,1)S(1)} %constant_dynamic-update-slice_fusion), kind=kLoop, calls=%fused_computation.20 | loop fusion | flops 10485760 | bytes 10485764 | tf_op jit(solution)/shard_map/jit(_roll_dynamic)/concatenate | solution.py:24
  140.9 1.7 fusion.13
  147.1 2.0 copy.45
  156.2 2.7 pad_maximum_fusion
  159.6 77.4 %reduce-scatter.3.cloned.1.call-done = bf16[32,5248]{1,0:T(8,128)(2,1)} async-done(((bf16[512,5248]{1,0:T(8,128)(2,1)}), bf16[32,5248]{1,0:T(8,128)(2,1)}) %reduce-scatter.3.cloned.1.call-update) | async-done | bytes 335888 | tf_op jit(solution)/shard_map/reduce_scatter | solution.py:101
  239.9 10.5 %collective-permute-done.16 = bf16[32,5120]{1,0:T(8,128)(2,1)S(1)} collective-permute-done((bf16[32,5120]{1,0:T(8,128)(2,1)S(1)}, bf16[32,5120]{1,0:T(8,128)(2,1)S(1)}, u32[]{:S(2)}, u32[]{:S(2)}) %collective-permute-start.16) | collective-permute-done | bytes 327712 | tf_op jit(solution)/shard_map/ppermute | solution.py:20
  250.4 5.3 %collective-permute-start.24 = (bf16[32,5120]{1,0:T(8,128)(2,1)S(1)}, bf16[32,5120]{1,0:T(8,128)(2,1)S(1)}, u32[]{:S(2)}, u32[]{:S(2)}) collective-permute-start(bf16[32,5120]{1,0:T(8,128)(2,1)S(1)} %multiply_convert_fusion.1), channel_id=1, source_target_pairs={{0,15},{1,0},{2,1},{3,2},{4,3},{5,4},{6,5},{7,6},{8,7},{9,8},{10,9... | collective-permute-start | bytes 983048 | tf_op jit(solution)/shard_map/ppermute | solution.py:22
  255.7 5.4 %collective-permute-done.17 = bf16[32,5120]{1,0:T(8,128)(2,1)S(1)} collective-permute-done((bf16[32,5120]{1,0:T(8,128)(2,1)S(1)}, bf16[32,5120]{1,0:T(8,128)(2,1)S(1)}, u32[]{:S(2)}, u32[]{:S(2)}) %collective-permute-start.17) | collective-permute-done | bytes 327712 | tf_op jit(solution)/shard_map/ppermute | solution.py:20
  261.1 5.3 %collective-permute-start.25 = (bf16[32,5120]{1,0:T(8,128)(2,1)S(1)}, bf16[32,5120]{1,0:T(8,128)(2,1)S(1)}, u32[]{:S(2)}, u32[]{:S(2)}) collective-permute-start(bf16[32,5120]{1,0:T(8,128)(2,1)S(1)} %collective-permute-done.24), channel_id=1, source_target_pairs={{0,15},{1,0},{2,1},{3,2},{4,3},{5,4},{6,5},{7,6},{8,7},{9,8},{10,9... | collective-permute-start | bytes 983048 | tf_op jit(solution)/shard_map/ppermute | solution.py:22
  266.5 5.0 %collective-permute-done.18 = bf16[32,5120]{1,0:T(8,128)(2,1)S(1)} collective-permute-done((bf16[32,5120]{1,0:T(8,128)(2,1)S(1)}, bf16[32,5120]{1,0:T(8,128)(2,1)S(1)}, u32[]{:S(2)}, u32[]{:S(2)}) %collective-permute-start.18) | collective-permute-done | bytes 327712 | tf_op jit(solution)/shard_map/ppermute | solution.py:20
  271.5 5.3 %collective-permute-start.26 = (bf16[32,5120]{1,0:T(8,128)(2,1)S(1)}, bf16[32,5120]{1,0:T(8,128)(2,1)S(1)}, u32[]{:S(2)}, u32[]{:S(2)}) collective-permute-start(bf16[32,5120]{1,0:T(8,128)(2,1)S(1)} %collective-permute-done.25), channel_id=1, source_target_pairs={{0,15},{1,0},{2,1},{3,2},{4,3},{5,4},{6,5},{7,6},{8,7},{9,8},{10,9... | collective-permute-start | bytes 983048 | tf_op jit(solution)/shard_map/ppermute | solution.py:22
  276.9 5.0 %collective-permute-done.19 = bf16[32,5120]{1,0:T(8,128)(2,1)S(1)} collective-permute-done((bf16[32,5120]{1,0:T(8,128)(2,1)S(1)}, bf16[32,5120]{1,0:T(8,128)(2,1)S(1)}, u32[]{:S(2)}, u32[]{:S(2)}) %collective-permute-start.19) | collective-permute-done | bytes 327712 | tf_op jit(solution)/shard_map/ppermute | solution.py:20
  282.6 4.7 collective-permute-start.27
  287.3 5.3 %collective-permute-done.20 = bf16[32,5120]{1,0:T(8,128)(2,1)} collective-permute-done((bf16[32,5120]{1,0:T(8,128)(2,1)S(1)}, bf16[32,5120]{1,0:T(8,128)(2,1)}, u32[]{:S(2)}, u32[]{:S(2)}) %collective-permute-start.20) | collective-permute-done | bytes 327712 | tf_op jit(solution)/shard_map/ppermute | solution.py:20
  292.8 5.6 %collective-permute-start.28 = (bf16[32,5120]{1,0:T(8,128)(2,1)S(1)}, bf16[32,5120]{1,0:T(8,128)(2,1)S(1)}, u32[]{:S(2)}, u32[]{:S(2)}) collective-permute-start(bf16[32,5120]{1,0:T(8,128)(2,1)S(1)} %collective-permute-done.27), channel_id=1, source_target_pairs={{0,15},{1,0},{2,1},{3,2},{4,3},{5,4},{6,5},{7,6},{8,7},{9,8},{10,9... | collective-permute-start | bytes 983048 | tf_op jit(solution)/shard_map/ppermute | solution.py:22
  298.4 6.3 %collective-permute-done.21 = bf16[32,5120]{1,0:T(8,128)(2,1)} collective-permute-done((bf16[32,5120]{1,0:T(8,128)(2,1)}, bf16[32,5120]{1,0:T(8,128)(2,1)}, u32[]{:S(2)}, u32[]{:S(2)}) %collective-permute-start.21) | collective-permute-done | bytes 327712 | tf_op jit(solution)/shard_map/ppermute | solution.py:20
  304.8 2.5 fusion.15
  307.3 26.8 %all_gather.14 = bf16[512,256]{1,0:T(8,128)(2,1)S(1)} all-gather(bf16[32,256]{1,0:T(8,128)(2,1)S(1)} %fusion.15), channel_id=1, replica_groups=mesh['req'=8,'mp'=16] {'mp'}, dimensions={0}, use_global_device_ids=true | all-gather | bytes 278528 | tf_op jit(solution)/shard_map/all_gather | solution.py:97
  334.1 2.1 collective-permute-start.29
  339.5 2.2 collective-permute-done.29
  341.7 4.9 %collective-permute-start.30 = (bf16[32,5120]{1,0:T(8,128)(2,1)S(1)}, bf16[32,5120]{1,0:T(8,128)(2,1)S(1)}, u32[]{:S(2)}, u32[]{:S(2)}) collective-permute-start(bf16[32,5120]{1,0:T(8,128)(2,1)S(1)} %collective-permute-done.29), channel_id=1, source_target_pairs={{0,15},{1,0},{2,1},{3,2},{4,3},{5,4},{6,5},{7,6},{8,7},{9,8},{10,9... | collective-permute-start | bytes 983048 | tf_op jit(solution)/shard_map/ppermute | solution.py:22
  348.1 1.7 constant_dynamic-update-slice_fusion.29
  349.9 1.7 constant_dynamic-update-slice_fusion.28
  360.8 8.3 %fusion.10 = f32[512,640]{1,0:T(8,128)S(1)} fusion(f32[512,640]{1,0:T(8,128)S(1)} %fusion.31, bf16[2,5120,640]{2,1,0:T(8,128)(2,1)} %all-gather.3.cloned.1.call-done, s32[]{:T(128)S(6)} %select_n.173, bf16[512,5120]{1,0:T(8,128)(2,1)} %constant_dynamic-update-slice_fusion.16), kind=kOutput, calls=%fused_computation.25 | convolution fusion | flops 3366256640 | bytes 14417924 | tf_op jit(solution)/shard_map/dot_general | solution.py:128
  369.1 7.1 %multiply_convert_fusion = bf16[512,640]{1,0:T(8,128)(2,1)S(1)} fusion(f32[512,640]{1,0:T(8,128)S(1)} %fusion.10, f32[512,640]{1,0:T(8,128)S(1)} %fusion.29, bf16[2,5120,640]{2,1,0:T(8,128)(2,1)S(1)} %copy-done.46, s32[]{:T(128)S(6)} %select_n.173, bf16[512,5120]{1,0:T(8,128)(2,1)} %constant_dynamic-update-slice_fusion.16), kind=kOutput, calls=%fused_computation.27 | convolution fusion | flops 3368222720 | bytes 15073284 | tf_op jit(solution)/shard_map/dot_general | solution.py:135
  376.6 7.4 %convolution_convert_fusion.1 = bf16[512,5120]{1,0:T(8,128)(2,1)S(1)} fusion(bf16[512,640]{1,0:T(8,128)(2,1)S(1)} %multiply_convert_fusion, bf16[5120,640]{1,0:T(8,128)(2,1)} %all-gather.5.cloned.1.call-done), kind=kOutput, calls=%fused_computation.5 | convolution fusion | flops 3358064640 | bytes 12451840 | tf_op jit(solution)/shard_map/dot_general | solution.py:143
  384.0 2.7 pad_maximum_fusion.1
  387.4 76.9 %reduce-scatter.5.cloned.1.call-done = bf16[32,5248]{1,0:T(8,128)(2,1)} async-done(((bf16[512,5248]{1,0:T(8,128)(2,1)}), bf16[32,5248]{1,0:T(8,128)(2,1)}) %reduce-scatter.5.cloned.1.call-update) | async-done | bytes 335888 | tf_op jit(solution)/shard_map/reduce_scatter | solution.py:101
  465.3 2.4 fusion.6
  (218 shorter events, 50.8 us)
Async XLA Ops:
  7.4 147.0 %copy-start = (bf16[256,5120]{1,0:T(8,128)(2,1)S(1)}, bf16[256,5120]{1,0:T(8,128)(2,1)}, u32[]{:S(2)}) copy-start(bf16[256,5120]{1,0:T(8,128)(2,1)} %param.29) | copy-start | bytes 7864324
  7.4 75.1 %copy-start.42 = (bf16[2,128,64]{1,2,0:T(8,128)(2,1)S(1)}, bf16[2,128,64]{1,2,0:T(8,128)(2,1)}, u32[]{:S(2)}) copy-start(bf16[2,128,64]{1,2,0:T(8,128)(2,1)} %param.32) | copy-start | bytes 98308
  7.4 229.6 %reduce-scatter.3.cloned.1.call-start = ((), (), s32[]{:S(2)}) async-start(), calls=%async_computation.2 | async-start | bytes 5709824 | tf_op jit(solution)/shard_map/reduce_scatter | solution.py:101
  9.8 13.1 %collective-permute-start = (bf16[32,5120]{1,0:T(8,128)(2,1)S(1)}, bf16[32,5120]{1,0:T(8,128)(2,1)S(1)}, u32[]{:S(2)}, u32[]{:S(2)}) collective-permute-start(bf16[32,5120]{1,0:T(8,128)(2,1)S(1)} %fusion.21), channel_id=1, source_target_pairs={{0,1},{1,2},{2,3},{3,4},{4,5},{5,6},{6,7},{7,8},{8,9},{9,10},{10,1... | collective-permute-start | bytes 983048 | tf_op jit(solution)/shard_map/ppermute | solution.py:20
  11.6 23.6 %collective-permute-start.8 = (bf16[32,5120]{1,0:T(8,128)(2,1)S(1)}, bf16[32,5120]{1,0:T(8,128)(2,1)}, u32[]{:S(2)}, u32[]{:S(2)}) collective-permute-start(bf16[32,5120]{1,0:T(8,128)(2,1)S(1)} %fusion.21), channel_id=1, source_target_pairs={{0,15},{1,0},{2,1},{3,2},{4,3},{5,4},{6,5},{7,6},{8,7},{9,8},{10,9... | collective-permute-start | bytes 983048 | tf_op jit(solution)/shard_map/ppermute | solution.py:22
  22.9 12.2 %collective-permute-start.1 = (bf16[32,5120]{1,0:T(8,128)(2,1)S(1)}, bf16[32,5120]{1,0:T(8,128)(2,1)S(1)}, u32[]{:S(2)}, u32[]{:S(2)}) collective-permute-start(bf16[32,5120]{1,0:T(8,128)(2,1)S(1)} %collective-permute-done), channel_id=1, source_target_pairs={{0,1},{1,2},{2,3},{3,4},{4,5},{5,6},{6,7},{7,8},{8,9},{9,10},{10,1... | collective-permute-start | bytes 983048 | tf_op jit(solution)/shard_map/ppermute | solution.py:20
  35.1 11.2 %collective-permute-start.2 = (bf16[32,5120]{1,0:T(8,128)(2,1)S(1)}, bf16[32,5120]{1,0:T(8,128)(2,1)S(1)}, u32[]{:S(2)}, u32[]{:S(2)}) collective-permute-start(bf16[32,5120]{1,0:T(8,128)(2,1)S(1)} %collective-permute-done.1), channel_id=1, source_target_pairs={{0,1},{1,2},{2,3},{3,4},{4,5},{5,6},{6,7},{7,8},{8,9},{9,10},{10,1... | collective-permute-start | bytes 983048 | tf_op jit(solution)/shard_map/ppermute | solution.py:20
  35.1 14.1 %collective-permute-start.9 = (bf16[32,5120]{1,0:T(8,128)(2,1)}, bf16[32,5120]{1,0:T(8,128)(2,1)S(1)}, u32[]{:S(2)}, u32[]{:S(2)}) collective-permute-start(bf16[32,5120]{1,0:T(8,128)(2,1)} %collective-permute-done.8), channel_id=1, source_target_pairs={{0,15},{1,0},{2,1},{3,2},{4,3},{5,4},{6,5},{7,6},{8,7},{9,8},{10,9... | collective-permute-start | bytes 983048 | tf_op jit(solution)/shard_map/ppermute | solution.py:22
  46.3 10.4 %collective-permute-start.3 = (bf16[32,5120]{1,0:T(8,128)(2,1)S(1)}, bf16[32,5120]{1,0:T(8,128)(2,1)S(1)}, u32[]{:S(2)}, u32[]{:S(2)}) collective-permute-start(bf16[32,5120]{1,0:T(8,128)(2,1)S(1)} %collective-permute-done.2), channel_id=1, source_target_pairs={{0,1},{1,2},{2,3},{3,4},{4,5},{5,6},{6,7},{7,8},{8,9},{9,10},{10,1... | collective-permute-start | bytes 983048 | tf_op jit(solution)/shard_map/ppermute | solution.py:20
  46.3 83.9 %copy-start.2 = (bf16[1,32,1,5120]{3,1,2,0:T(8,128)(2,1)S(1)}, bf16[1,32,1,5120]{3,1,2,0:T(8,128)(2,1)}, u32[]{:S(2)}) copy-start(bf16[1,32,1,5120]{3,1,2,0:T(8,128)(2,1)} %param.22) | copy-start | bytes 983044
  46.4 83.9 %copy-start.39 = (f32[5120]{0:T(1024)S(1)}, f32[5120]{0:T(1024)}, u32[]{:S(2)}) copy-start(f32[5120]{0:T(1024)} %param.25) | copy-start | bytes 61444
  49.3 33.4 %collective-permute-start.10 = (bf16[32,5120]{1,0:T(8,128)(2,1)S(1)}, bf16[32,5120]{1,0:T(8,128)(2,1)S(1)}, u32[]{:S(2)}, u32[]{:S(2)}) collective-permute-start(bf16[32,5120]{1,0:T(8,128)(2,1)S(1)} %collective-permute-done.9), channel_id=1, source_target_pairs={{0,15},{1,0},{2,1},{3,2},{4,3},{5,4},{6,5},{7,6},{8,7},{9,8},{10,9... | collective-permute-start | bytes 983048 | tf_op jit(solution)/shard_map/ppermute | solution.py:22
  56.7 30.6 %collective-permute-start.4 = (bf16[32,5120]{1,0:T(8,128)(2,1)S(1)}, bf16[32,5120]{1,0:T(8,128)(2,1)S(1)}, u32[]{:S(2)}, u32[]{:S(2)}) collective-permute-start(bf16[32,5120]{1,0:T(8,128)(2,1)S(1)} %collective-permute-done.3), channel_id=1, source_target_pairs={{0,1},{1,2},{2,3},{3,4},{4,5},{5,6},{6,7},{7,8},{8,9},{9,10},{10,1... | collective-permute-start | bytes 983048 | tf_op jit(solution)/shard_map/ppermute | solution.py:20
  82.7 11.2 %collective-permute-start.11 = (bf16[32,5120]{1,0:T(8,128)(2,1)S(1)}, bf16[32,5120]{1,0:T(8,128)(2,1)S(1)}, u32[]{:S(2)}, u32[]{:S(2)}) collective-permute-start(bf16[32,5120]{1,0:T(8,128)(2,1)S(1)} %collective-permute-done.10), channel_id=1, source_target_pairs={{0,15},{1,0},{2,1},{3,2},{4,3},{5,4},{6,5},{7,6},{8,7},{9,8},{10,9... | collective-permute-start | bytes 983048 | tf_op jit(solution)/shard_map/ppermute | solution.py:22
  87.3 12.3 %collective-permute-start.5 = (bf16[32,5120]{1,0:T(8,128)(2,1)S(1)}, bf16[32,5120]{1,0:T(8,128)(2,1)S(1)}, u32[]{:S(2)}, u32[]{:S(2)}) collective-permute-start(bf16[32,5120]{1,0:T(8,128)(2,1)S(1)} %collective-permute-done.4), channel_id=1, source_target_pairs={{0,1},{1,2},{2,3},{3,4},{4,5},{5,6},{6,7},{7,8},{8,9},{9,10},{10,1... | collective-permute-start | bytes 983048 | tf_op jit(solution)/shard_map/ppermute | solution.py:20
  93.8 11.6 %collective-permute-start.12 = (bf16[32,5120]{1,0:T(8,128)(2,1)S(1)}, bf16[32,5120]{1,0:T(8,128)(2,1)}, u32[]{:S(2)}, u32[]{:S(2)}) collective-permute-start(bf16[32,5120]{1,0:T(8,128)(2,1)S(1)} %collective-permute-done.11), channel_id=1, source_target_pairs={{0,15},{1,0},{2,1},{3,2},{4,3},{5,4},{6,5},{7,6},{8,7},{9,8},{10,9... | collective-permute-start | bytes 983048 | tf_op jit(solution)/shard_map/ppermute | solution.py:22
  99.7 11.7 %collective-permute-start.6 = (bf16[32,5120]{1,0:T(8,128)(2,1)S(1)}, bf16[32,5120]{1,0:T(8,128)(2,1)}, u32[]{:S(2)}, u32[]{:S(2)}) collective-permute-start(bf16[32,5120]{1,0:T(8,128)(2,1)S(1)} %collective-permute-done.5), channel_id=1, source_target_pairs={{0,1},{1,2},{2,3},{3,4},{4,5},{5,6},{6,7},{7,8},{8,9},{9,10},{10,1... | collective-permute-start | bytes 983048 | tf_op jit(solution)/shard_map/ppermute | solution.py:20
  105.5 11.5 %collective-permute-start.13 = (bf16[32,5120]{1,0:T(8,128)(2,1)}, bf16[32,5120]{1,0:T(8,128)(2,1)}, u32[]{:S(2)}, u32[]{:S(2)}) collective-permute-start(bf16[32,5120]{1,0:T(8,128)(2,1)} %collective-permute-done.12), channel_id=1, source_target_pairs={{0,15},{1,0},{2,1},{3,2},{4,3},{5,4},{6,5},{7,6},{8,7},{9,8},{10,9... | collective-permute-start | bytes 983048 | tf_op jit(solution)/shard_map/ppermute | solution.py:22
  111.4 11.9 %collective-permute-start.7 = (bf16[32,5120]{1,0:T(8,128)(2,1)}, bf16[32,5120]{1,0:T(8,128)(2,1)}, u32[]{:S(2)}, u32[]{:S(2)}) collective-permute-start(bf16[32,5120]{1,0:T(8,128)(2,1)} %collective-permute-done.6), channel_id=1, source_target_pairs={{0,1},{1,2},{2,3},{3,4},{4,5},{5,6},{6,7},{7,8},{8,9},{9,10},{10,1... | collective-permute-start | bytes 983048 | tf_op jit(solution)/shard_map/ppermute | solution.py:20
  117.0 17.2 %collective-permute-start.14 = (bf16[32,5120]{1,0:T(8,128)(2,1)}, bf16[32,5120]{1,0:T(8,128)(2,1)S(1)}, u32[]{:S(2)}, u32[]{:S(2)}) collective-permute-start(bf16[32,5120]{1,0:T(8,128)(2,1)} %collective-permute-done.13), channel_id=1, source_target_pairs={{0,15},{1,0},{2,1},{3,2},{4,3},{5,4},{6,5},{7,6},{8,7},{9,8},{10,9... | collective-permute-start | bytes 983048 | tf_op jit(solution)/shard_map/ppermute | solution.py:22
  143.3 7.1 %collective-permute-start.15 = (bf16[2,512,64]{1,2,0:T(8,128)(2,1)}, bf16[2,512,64]{1,2,0:T(8,128)(2,1)}, u32[]{:S(2)}, u32[]{:S(2)}) collective-permute-start(bf16[2,512,64]{1,2,0:T(8,128)(2,1)} %maximum_convert_fusion), channel_id=1, source_target_pairs={{0,1},{1,0},{2,3},{3,2},{4,5},{5,4},{6,7},{7,6},{8,9},{9,8},{10,11... | collective-permute-start | bytes 393224 | tf_op jit(solution)/shard_map/ppermute | solution.py:28
  158.9 79.1 %copy-start.3 = (bf16[1,32,1,5120]{3,1,2,0:T(8,128)(2,1)S(1)}, bf16[1,32,1,5120]{3,1,2,0:T(8,128)(2,1)}, u32[]{:S(2)}) copy-start(bf16[1,32,1,5120]{3,1,2,0:T(8,128)(2,1)} %param.22) | copy-start | bytes 983044
  158.9 79.1 %copy-start.4 = (bf16[128,5120]{1,0:T(8,128)(2,1)S(1)}, bf16[128,5120]{1,0:T(8,128)(2,1)}, u32[]{:S(2)}) copy-start(bf16[128,5120]{1,0:T(8,128)(2,1)} %param.34) | copy-start | bytes 3932164
  158.9 79.6 %copy-start.40 = (f32[5120]{0:T(1024)S(1)}, f32[5120]{0:T(1024)}, u32[]{:S(2)}) copy-start(f32[5120]{0:T(1024)} %param.35) | copy-start | bytes 61444
  158.9 201.8 %all-gather.3.cloned.1.call-start = ((), (), s32[]{:S(2)}) async-start(), calls=%async_computation.3 | async-start | bytes 14745600 | tf_op jit(solution)/shard_map/all_gather | solution.py:196
  159.5 217.1 %all-gather.5.cloned.1.call-start = ((), (), s32[]{:S(2)}) async-start(), calls=%async_computation.4 | async-start | bytes 7372800 | tf_op jit(solution)/shard_map/all_gather | solution.py:197
  238.6 11.7 %collective-permute-start.16 = (bf16[32,5120]{1,0:T(8,128)(2,1)S(1)}, bf16[32,5120]{1,0:T(8,128)(2,1)S(1)}, u32[]{:S(2)}, u32[]{:S(2)}) collective-permute-start(bf16[32,5120]{1,0:T(8,128)(2,1)S(1)} %multiply_convert_fusion.1), channel_id=1, source_target_pairs={{0,1},{1,2},{2,3},{3,4},{4,5},{5,6},{6,7},{7,8},{8,9},{9,10},{10,1... | collective-permute-start | bytes 983048 | tf_op jit(solution)/shard_map/ppermute | solution.py:20
  250.4 86.4 %copy-start.21 = (bf16[32,5120]{1,0:T(8,128)(2,1)}, bf16[32,5120]{1,0:T(8,128)(2,1)S(1)}, u32[]{:S(2)}) copy-start(bf16[32,5120]{1,0:T(8,128)(2,1)S(1)} %collective-permute-done.16) | copy-start | bytes 983044
  250.4 10.7 %collective-permute-start.17 = (bf16[32,5120]{1,0:T(8,128)(2,1)S(1)}, bf16[32,5120]{1,0:T(8,128)(2,1)S(1)}, u32[]{:S(2)}, u32[]{:S(2)}) collective-permute-start(bf16[32,5120]{1,0:T(8,128)(2,1)S(1)} %collective-permute-done.16), channel_id=1, source_target_pairs={{0,1},{1,2},{2,3},{3,4},{4,5},{5,6},{6,7},{7,8},{8,9},{9,10},{10,1... | collective-permute-start | bytes 983048 | tf_op jit(solution)/shard_map/ppermute | solution.py:20
  250.4 10.8 %collective-permute-start.24 = (bf16[32,5120]{1,0:T(8,128)(2,1)S(1)}, bf16[32,5120]{1,0:T(8,128)(2,1)S(1)}, u32[]{:S(2)}, u32[]{:S(2)}) collective-permute-start(bf16[32,5120]{1,0:T(8,128)(2,1)S(1)} %multiply_convert_fusion.1), channel_id=1, source_target_pairs={{0,15},{1,0},{2,1},{3,2},{4,3},{5,4},{6,5},{7,6},{8,7},{9,8},{10,9... | collective-permute-start | bytes 983048 | tf_op jit(solution)/shard_map/ppermute | solution.py:22
  261.1 75.7 %copy-start.25 = (bf16[32,5120]{1,0:T(8,128)(2,1)}, bf16[32,5120]{1,0:T(8,128)(2,1)S(1)}, u32[]{:S(2)}) copy-start(bf16[32,5120]{1,0:T(8,128)(2,1)S(1)} %collective-permute-done.17) | copy-start | bytes 983044
  261.1 10.4 %collective-permute-start.18 = (bf16[32,5120]{1,0:T(8,128)(2,1)S(1)}, bf16[32,5120]{1,0:T(8,128)(2,1)S(1)}, u32[]{:S(2)}, u32[]{:S(2)}) collective-permute-start(bf16[32,5120]{1,0:T(8,128)(2,1)S(1)} %collective-permute-done.17), channel_id=1, source_target_pairs={{0,1},{1,2},{2,3},{3,4},{4,5},{5,6},{6,7},{7,8},{8,9},{9,10},{10,1... | collective-permute-start | bytes 983048 | tf_op jit(solution)/shard_map/ppermute | solution.py:20
  261.1 75.7 %copy-start.23 = (bf16[32,5120]{1,0:T(8,128)(2,1)}, bf16[32,5120]{1,0:T(8,128)(2,1)S(1)}, u32[]{:S(2)}) copy-start(bf16[32,5120]{1,0:T(8,128)(2,1)S(1)} %collective-permute-done.24) | copy-start | bytes 983044
  261.1 10.4 %collective-permute-start.25 = (bf16[32,5120]{1,0:T(8,128)(2,1)S(1)}, bf16[32,5120]{1,0:T(8,128)(2,1)S(1)}, u32[]{:S(2)}, u32[]{:S(2)}) collective-permute-start(bf16[32,5120]{1,0:T(8,128)(2,1)S(1)} %collective-permute-done.24), channel_id=1, source_target_pairs={{0,15},{1,0},{2,1},{3,2},{4,3},{5,4},{6,5},{7,6},{8,7},{9,8},{10,9... | collective-permute-start | bytes 983048 | tf_op jit(solution)/shard_map/ppermute | solution.py:22
  271.5 64.6 %copy-start.30 = (bf16[32,5120]{1,0:T(8,128)(2,1)}, bf16[32,5120]{1,0:T(8,128)(2,1)S(1)}, u32[]{:S(2)}) copy-start(bf16[32,5120]{1,0:T(8,128)(2,1)S(1)} %collective-permute-done.18) | copy-start | bytes 983044
  271.5 10.4 %collective-permute-start.19 = (bf16[32,5120]{1,0:T(8,128)(2,1)S(1)}, bf16[32,5120]{1,0:T(8,128)(2,1)S(1)}, u32[]{:S(2)}, u32[]{:S(2)}) collective-permute-start(bf16[32,5120]{1,0:T(8,128)(2,1)S(1)} %collective-permute-done.18), channel_id=1, source_target_pairs={{0,1},{1,2},{2,3},{3,4},{4,5},{5,6},{6,7},{7,8},{8,9},{9,10},{10,1... | collective-permute-start | bytes 983048 | tf_op jit(solution)/shard_map/ppermute | solution.py:20
  271.5 64.6 %copy-start.28 = (bf16[32,5120]{1,0:T(8,128)(2,1)}, bf16[32,5120]{1,0:T(8,128)(2,1)S(1)}, u32[]{:S(2)}) copy-start(bf16[32,5120]{1,0:T(8,128)(2,1)S(1)} %collective-permute-done.25) | copy-start | bytes 983044
  271.5 10.4 %collective-permute-start.26 = (bf16[32,5120]{1,0:T(8,128)(2,1)S(1)}, bf16[32,5120]{1,0:T(8,128)(2,1)S(1)}, u32[]{:S(2)}, u32[]{:S(2)}) collective-permute-start(bf16[32,5120]{1,0:T(8,128)(2,1)S(1)} %collective-permute-done.25), channel_id=1, source_target_pairs={{0,15},{1,0},{2,1},{3,2},{4,3},{5,4},{6,5},{7,6},{8,7},{9,8},{10,9... | collective-permute-start | bytes 983048 | tf_op jit(solution)/shard_map/ppermute | solution.py:22
  281.9 10.8 %collective-permute-start.20 = (bf16[32,5120]{1,0:T(8,128)(2,1)S(1)}, bf16[32,5120]{1,0:T(8,128)(2,1)}, u32[]{:S(2)}, u32[]{:S(2)}) collective-permute-start(bf16[32,5120]{1,0:T(8,128)(2,1)S(1)} %collective-permute-done.19), channel_id=1, source_target_pairs={{0,1},{1,2},{2,3},{3,4},{4,5},{5,6},{6,7},{7,8},{8,9},{9,10},{10,1... | collective-permute-start | bytes 983048 | tf_op jit(solution)/shard_map/ppermute | solution.py:20
  282.6 10.1 %collective-permute-start.27 = (bf16[32,5120]{1,0:T(8,128)(2,1)S(1)}, bf16[32,5120]{1,0:T(8,128)(2,1)S(1)}, u32[]{:S(2)}, u32[]{:S(2)}) collective-permute-start(bf16[32,5120]{1,0:T(8,128)(2,1)S(1)} %collective-permute-done.26), channel_id=1, source_target_pairs={{0,15},{1,0},{2,1},{3,2},{4,3},{5,4},{6,5},{7,6},{8,7},{9,8},{10,9... | collective-permute-start | bytes 983048 | tf_op jit(solution)/shard_map/ppermute | solution.py:22
  292.7 12.0 %collective-permute-start.21 = (bf16[32,5120]{1,0:T(8,128)(2,1)}, bf16[32,5120]{1,0:T(8,128)(2,1)}, u32[]{:S(2)}, u32[]{:S(2)}) collective-permute-start(bf16[32,5120]{1,0:T(8,128)(2,1)} %collective-permute-done.20), channel_id=1, source_target_pairs={{0,1},{1,2},{2,3},{3,4},{4,5},{5,6},{6,7},{7,8},{8,9},{9,10},{10,1... | collective-permute-start | bytes 983048 | tf_op jit(solution)/shard_map/ppermute | solution.py:20
  292.7 171.6 %reduce-scatter.5.cloned.1.call-start = ((), (), s32[]{:S(2)}) async-start(), calls=%async_computation.5 | async-start | bytes 5709824 | tf_op jit(solution)/shard_map/reduce_scatter | solution.py:101
  292.8 41.3 %collective-permute-start.28 = (bf16[32,5120]{1,0:T(8,128)(2,1)S(1)}, bf16[32,5120]{1,0:T(8,128)(2,1)S(1)}, u32[]{:S(2)}, u32[]{:S(2)}) collective-permute-start(bf16[32,5120]{1,0:T(8,128)(2,1)S(1)} %collective-permute-done.27), channel_id=1, source_target_pairs={{0,15},{1,0},{2,1},{3,2},{4,3},{5,4},{6,5},{7,6},{8,7},{9,8},{10,9... | collective-permute-start | bytes 983048 | tf_op jit(solution)/shard_map/ppermute | solution.py:22
  304.7 31.4 %collective-permute-start.22 = (bf16[32,5120]{1,0:T(8,128)(2,1)}, bf16[32,5120]{1,0:T(8,128)(2,1)S(1)}, u32[]{:S(2)}, u32[]{:S(2)}) collective-permute-start(bf16[32,5120]{1,0:T(8,128)(2,1)} %collective-permute-done.21), channel_id=1, source_target_pairs={{0,1},{1,2},{2,3},{3,4},{4,5},{5,6},{6,7},{7,8},{8,9},{9,10},{10,1... | collective-permute-start | bytes 983048 | tf_op jit(solution)/shard_map/ppermute | solution.py:20
  334.1 7.6 %collective-permute-start.29 = (bf16[32,5120]{1,0:T(8,128)(2,1)S(1)}, bf16[32,5120]{1,0:T(8,128)(2,1)S(1)}, u32[]{:S(2)}, u32[]{:S(2)}) collective-permute-start(bf16[32,5120]{1,0:T(8,128)(2,1)S(1)} %collective-permute-done.28), channel_id=1, source_target_pairs={{0,15},{1,0},{2,1},{3,2},{4,3},{5,4},{6,5},{7,6},{8,7},{9,8},{10,9... | collective-permute-start | bytes 983048 | tf_op jit(solution)/shard_map/ppermute | solution.py:22
  336.2 10.5 %collective-permute-start.23 = (bf16[32,5120]{1,0:T(8,128)(2,1)S(1)}, bf16[32,5120]{1,0:T(8,128)(2,1)S(1)}, u32[]{:S(2)}, u32[]{:S(2)}) collective-permute-start(bf16[32,5120]{1,0:T(8,128)(2,1)S(1)} %collective-permute-done.22), channel_id=1, source_target_pairs={{0,1},{1,2},{2,3},{3,4},{4,5},{5,6},{6,7},{7,8},{8,9},{9,10},{10,1... | collective-permute-start | bytes 983048 | tf_op jit(solution)/shard_map/ppermute | solution.py:20
  341.7 18.3 %collective-permute-start.30 = (bf16[32,5120]{1,0:T(8,128)(2,1)S(1)}, bf16[32,5120]{1,0:T(8,128)(2,1)S(1)}, u32[]{:S(2)}, u32[]{:S(2)}) collective-permute-start(bf16[32,5120]{1,0:T(8,128)(2,1)S(1)} %collective-permute-done.29), channel_id=1, source_target_pairs={{0,15},{1,0},{2,1},{3,2},{4,3},{5,4},{6,5},{7,6},{8,7},{9,8},{10,9... | collective-permute-start | bytes 983048 | tf_op jit(solution)/shard_map/ppermute | solution.py:22
  384.0 83.7 %copy-start.1 = (bf16[256,5120]{1,0:T(8,128)(2,1)S(1)}, bf16[256,5120]{1,0:T(8,128)(2,1)}, u32[]{:S(2)}) copy-start(bf16[256,5120]{1,0:T(8,128)(2,1)} %param.29) | copy-start | bytes 7864324
  (35 other events, 594.0 us)
Sparse Core Ops, SparseCore 0:
  159.1 77.8 reduce-scatter.2
  386.9 77.3 reduce-scatter.4
Sparse Core Ops, SparseCore 1:
  161.1 68.1 all-gather.2
  292.8 43.2 all-gather.4
